TPU v7x, 32 devices: a whole 2x2x4 slice. The times are simulated.
32 devices in a mesh: seq: 8 (over z, y), fsdp: 4 (over x, core).
Axes of the slice: x: 2, y: 2, z: 4, core: 2. Of those that a mesh axis runs over, the one named last changes fastest.
Arguments:
- inputs: bfloat16 [12288, 1536], P(('seq', 'fsdp')), may hold values from -15 to 15
- layer_norm_gain: float32 [1536], replicated, may hold values from 0.25 to 1.75
- layer_norm_bias: float32 [1536], replicated, may hold values from -4 to 4
- w_in: bfloat16 [1536, 3072], P('fsdp'), may hold values from -0.15625 to 0.15625
- dw_kernel: float32 [32, 1536], replicated, may hold values from -1 to 1
- bn_gain: float32 [1536], replicated, may hold values from 0.25 to 1.75
- bn_bias: float32 [1536], replicated, may hold values from -4 to 4
- cotangent: bfloat16 [12288, 1536], P(('seq', 'fsdp')), may hold values from -6 to 6
Outputs:
- output: bfloat16 [12288, 1536], P(('seq', 'fsdp'))
- input_gradient: bfloat16 [12288, 1536], P(('seq', 'fsdp'))
- grad_w_in: float32 [1536, 3072], P('fsdp')
- grad_kernel: float32 [32, 1536], replicated
- grad_bn_gain: float32 [1536], replicated
- grad_bn_bias: float32 [1536], replicated
- layer_norm_gain_gradient: float32 [1536], replicated
- grad_ln_bias: float32 [1536], replicated
All inputs are finite; a program needn't handle non-finite values.
Results may differ from a plain program's by a relative error of at most 0.012.
The roundings to bfloat16 on the way count: a program that leaves them out, or rounds other values in their place, can miss the bound.
Values may be sent and summed in bfloat16 or wider, within the bound.
No kernel may reach another device: no remote copies, remote signals or barrier semaphores. Data moves between devices by JAX's collectives and lax.ppermute only.
A program may use at most 128 MiB of HBM per device.

v0:
```python
import jax
import jax.numpy as jnp
from jax import lax
from jax.sharding import PartitionSpec as P

epsilon = 1e-05


def from_behind(block, axis, distance):
    devices = range(lax.axis_size(axis))
    route = [(i - distance, i) for i in devices if i - distance in devices]
    return lax.ppermute(block, axis, route)


def on_device(
    inputs, layer_norm_gain, layer_norm_bias, w_in, dw_kernel, bn_gain, bn_bias, cotangent
):
    tok_rows = inputs.shape[0]
    features = inputs.shape[1]
    kernel_len = dw_kernel.shape[0]
    all_frames = tok_rows * lax.axis_size("seq") * lax.axis_size("fsdp")
    frames = inputs.astype(jnp.float32)
    row_mean = jnp.mean(frames, axis=-1, keepdims=True)
    centered_rows = frames - row_mean
    row_inverse_deviation = lax.rsqrt(
        jnp.mean(centered_rows * centered_rows, axis=-1, keepdims=True) + epsilon
    )
    standardized_input = centered_rows * row_inverse_deviation
    normalized_rows = (standardized_input * layer_norm_gain + layer_norm_bias).astype(jnp.bfloat16)
    full_weight = lax.all_gather(w_in, "fsdp", axis=0, tiled=True)
    hidden = jnp.dot(normalized_rows, full_weight, preferred_element_type=jnp.float32)
    value_part = hidden[:, :features]
    gate_sig = jax.nn.sigmoid(hidden[:, features:])
    glu = (value_part * gate_sig).astype(jnp.bfloat16)
    past_rim = from_behind(glu[tok_rows - (kernel_len - 1) :], ("seq", "fsdp"), 1)
    padded_glu = jnp.concatenate([past_rim, glu], axis=0).astype(jnp.float32)
    conv_out = jnp.zeros((tok_rows, features), jnp.float32)
    for offset in range(kernel_len):
        conv_out = (
            conv_out
            + dw_kernel[offset]
            * padded_glu[kernel_len - 1 - offset : kernel_len - 1 - offset + tok_rows]
        )
    chan_mean = lax.psum(jnp.sum(conv_out, axis=0), ("seq", "fsdp")) / all_frames
    conv_centred = conv_out - chan_mean
    chan_var = lax.psum(jnp.sum(conv_centred * conv_centred, axis=0), ("seq", "fsdp")) / all_frames
    bn_rstd = lax.rsqrt(chan_var + epsilon)
    chat = conv_centred * bn_rstd
    z_value = chat * bn_gain + bn_bias
    z_sig = jax.nn.sigmoid(z_value)
    output = (z_value * z_sig).astype(jnp.bfloat16)
    grad_z = cotangent.astype(jnp.float32) * z_sig * (1.0 + z_value * (1.0 - z_sig))
    grad_bn_bias, grad_bn_gain = lax.psum(
        (jnp.sum(grad_z, axis=0), jnp.sum(grad_z * chat, axis=0)), ("seq", "fsdp")
    )
    grad_conv = (
        bn_gain * bn_rstd * (grad_z - grad_bn_bias / all_frames - chat * grad_bn_gain / all_frames)
    )
    future_rim = from_behind(grad_conv[: kernel_len - 1], ("seq", "fsdp"), -1)
    padded_grad = jnp.concatenate([grad_conv, future_rim], axis=0)
    grad_glu = jnp.zeros((tok_rows, features), jnp.float32)
    kernel_rows = []
    for offset in range(kernel_len):
        grad_glu = grad_glu + dw_kernel[offset] * padded_grad[offset : offset + tok_rows]
        kernel_rows.append(
            jnp.sum(
                grad_conv
                * padded_glu[kernel_len - 1 - offset : kernel_len - 1 - offset + tok_rows],
                axis=0,
            )
        )
    kernel_portion = jnp.stack(kernel_rows, axis=0)
    grad_value = grad_glu * gate_sig
    grad_gate = grad_glu * value_part * gate_sig * (1.0 - gate_sig)
    grad_hidden = jnp.concatenate([grad_value, grad_gate], axis=1).astype(jnp.bfloat16)
    normalized_gradient = lax.dot_general(
        grad_hidden, full_weight, (((1,), (1,)), ((), ())), preferred_element_type=jnp.float32
    )
    grad_kernel, layer_norm_gain_gradient, grad_ln_bias = lax.psum(
        (
            kernel_portion,
            jnp.sum(normalized_gradient * standardized_input, axis=0),
            jnp.sum(normalized_gradient, axis=0),
        ),
        ("seq", "fsdp"),
    )
    rescaled_rows = normalized_gradient * layer_norm_gain
    input_gradient = row_inverse_deviation * (
        rescaled_rows
        - jnp.mean(rescaled_rows, axis=-1, keepdims=True)
        - standardized_input * jnp.mean(rescaled_rows * standardized_input, axis=-1, keepdims=True)
    )
    row_share = lax.psum_scatter(
        lax.dot_general(
            normalized_rows,
            grad_hidden,
            (((0,), (0,)), ((), ())),
            preferred_element_type=jnp.float32,
        ),
        "fsdp",
        scatter_dimension=0,
        tiled=True,
    )
    grad_w_in = lax.psum(row_share, "seq")
    return (
        output,
        input_gradient.astype(jnp.bfloat16),
        grad_w_in,
        grad_kernel,
        grad_bn_gain,
        grad_bn_bias,
        layer_norm_gain_gradient,
        grad_ln_bias,
    )


def solution(mesh):
    placed = (
        P(("seq", "fsdp"), None),
        P(),
        P(),
        P("fsdp", None),
        P(),
        P(),
        P(),
        P(("seq", "fsdp"), None),
    )
    return jax.shard_map(
        on_device,
        mesh=mesh,
        in_specs=placed,
        out_specs=(
            P(("seq", "fsdp"), None),
            P(("seq", "fsdp"), None),
            P("fsdp", None),
            P(),
            P(),
            P(),
            P(),
            P(),
        ),
        check_vma=False,
    )
```

profile of v0, /device:TPU:0, one launch (start us, length us, event | category | flops | bytes accessed | tf_op | source)
XLA Modules:
  0.0 759.2 jit_solution(17330102155597915595)
XLA Ops:
  7.2 0.0 copy-start.10
  7.2 0.0 copy-start.2
  7.2 0.0 copy-start.11
  7.2 0.0 copy-start.12
  7.2 0.0 all-gather.2.cloned.1.call-start
  7.3 0.7 all-gather.2.cloned.1.call-update
  7.9 0.0 reduce-scatter.2.cloned.1.call-start
  8.0 0.1 copy-done.10
  8.1 0.3 slice_reduce_fusion.31
  8.4 0.2 copy-done.2
  8.6 0.2 convert_reduce_fusion
  8.8 0.4 fusion.13
  9.3 67.3 %all-gather.2.cloned.1.call-done = bf16[1536,3072]{1,0:T(8,128)(2,1)} async-done(((bf16[384,3072]{1,0:T(8,128)(2,1)}), bf16[1536,3072]{1,0:T(8,128)(2,1)}) %all-gather.2.cloned.1.call-update) | async-done | bytes 9437200 | tf_op jit(solution)/shard_map/all_gather | solution.py:30
  76.6 0.0 copy-done.11
  76.6 0.0 copy-done.12
  76.6 6.7 fusion.115
  83.2 0.0 copy-start
  83.3 0.6 multiply_convert_fusion.3
  83.9 1.5 copy-done
  85.5 2.2 collective-permute-start
  87.7 0.2 slice_reduce_fusion.30
  87.9 0.7 collective-permute-done
  88.6 0.3 maximum_convert_fusion
  88.9 10.2 %fusion.119 = (f32[1536]{0:T(1024)S(1)}, f32[384,1536]{1,0:T(8,128)}) fusion(f32[415,1536]{1,0:T(8,128)S(1)} %maximum_convert_fusion, f32[1536]{0:T(1024)S(1)} %get-tuple-element.76, f32[1536]{0:T(1024)S(1)} %get-tuple-element.77, f32[1536]{0:T(1024)S(1)} %get-tuple-element.47, f32[1536]{0:T(1024)S(1)} %get-tuple-element.48, ...), kind=kLoop, calls=%fused_computation.261 | loop fusion | flops 37747200 | bytes 78059520 | tf_op jit(solution)/shard_map/reduce_sum | solution.py:44
  99.1 44.0 %psum.56 = f32[1536]{0:T(1024)S(1)} all-reduce(f32[1536]{0:T(1024)S(1)} %get-tuple-element.85), channel_id=1, replica_groups=mesh['seq'=8,'fsdp'=4] {'seq','fsdp'}, use_global_device_ids=true, to_apply=%region_3.0 | all-reduce | flops 1536 | bytes 12288 | tf_op jit(solution)/shard_map/psum | solution.py:44
  143.2 1.9 multiply_reduce_fusion.33
  145.1 40.1 %psum.57 = f32[1536]{0:T(1024)S(1)} all-reduce(f32[1536]{0:T(1024)S(1)} %multiply_reduce_fusion.33), channel_id=1, replica_groups=mesh['seq'=8,'fsdp'=4] {'seq','fsdp'}, use_global_device_ids=true, to_apply=%region_5.0 | all-reduce | flops 1536 | bytes 12288 | tf_op jit(solution)/shard_map/psum | solution.py:46
  185.2 0.0 copy-done.13
  185.2 0.0 copy-done.14
  185.3 4.5 fusion.117
  189.7 40.2 %all-reduce.1 = (f32[1536]{0:T(1024)S(1)}, f32[1536]{0:T(1024)S(1)}) all-reduce(f32[1536]{0:T(1024)S(1)} %get-tuple-element.41, f32[1536]{0:T(1024)S(1)} %get-tuple-element.40), channel_id=1, replica_groups=mesh['seq'=8,'fsdp'=4] {'seq','fsdp'}, use_global_device_ids=true, to_apply=%region_9.0 | all-reduce | flops 3072 | bytes 24576 | tf_op jit(solution)/shard_map/psum | solution.py:53
  230.0 0.6 copy-done.16
  230.5 8.2 %multiply_reduce_fusion = (f32[1536]{0:T(1024)S(1)}, f32[1536]{0:T(1024)S(1)}, f32[1536]{0:T(1024)S(1)}, f32[1536]{0:T(1024)S(1)}, f32[1536]{0:T(1024)S(1)}, /*i...) fusion(f32[415,1536]{1,0:T(8,128)S(1)} %maximum_convert_fusion,, ...), kind=kLoop, calls=%fused_computation.169 | loop fusion | flops 31822848 | bytes 48519168 | tf_op jit(solution)/shard_map/reduce_sum | solution.py:66
  238.8 0.0 copy-done.15
  238.8 0.0 copy-start.1
  238.8 1.4 copy-done.1
  240.2 1.5 collective-permute-start.1
  241.7 1.9 collective-permute-done.1
  243.5 40.4 %multiply_convert_fusion.1 = (bf16[384,1536]{1,0:T(8,128)(2,1)S(1)}, f32[384,1536]{1,0:T(8,128)}) fusion(f32[384,3072]{1,0:T(8,128)} %copy-done, f32[31,1536]{1,0:T(8,128)S(1)} %collective-permute-done.1, f32[384,1536]{1,0:T(8,128)} %copy-done.1, f32[1536]{0:T(1024)S(1)} %get-tuple-element.76, f32[1536]{0:T(1024)S(1)} %get-tuple-element.77, ...), kind=kLoop, calls=%fused_computation.202 | loop fusion | flops 58392576 | bytes 8644608 | tf_op jit(solution)/shard_map/convert
  283.9 0.0 copy-start.3
  284.0 4.4 multiply_convert_fusion
  288.4 0.0 copy-start.7
  288.4 0.0 copy-done.5
  288.4 1.0 copy-done.7
  289.4 9.4 %fusion.109 = f32[1536,3072]{1,0:T(8,128)} fusion(bf16[384,1536]{1,0:T(8,128)(2,1)S(1)} %multiply_convert_fusion, bf16[384,1536]{1,0:T(8,128)(2,1)S(1)} %get-tuple-element.83, bf16[384,1536]{1,0:T(8,128)(2,1)S(1)} %copy-done.3, f32[1536]{0:T(1024)S(1)} %copy-done.12, f32[1536]{0:T(1024)S(1)} %copy-done.11, f32[384]{0:T(512)S(1)} %add_rsqrt_fusion.1, ...), kind=kOutput, calls=%fused_computation.214 | convolution fusion | flops 3632136192 | bytes 22428672 | tf_op jit(solution)/shard_map/dot_general | solution.py:94
  298.8 0.0 reduce-scatter.2.cloned.1.call-update
  298.8 0.0 all-reduce.7.cloned.1.call-start
  298.9 5.4 multiply_reduce_fusion.18
  304.8 2.8 stack.131
  307.6 0.0 all-reduce.7.cloned.1.call-update
  307.6 0.3 all-reduce.5.cloned.1.call-start
  307.9 134.5 %reduce-scatter.2.cloned.1.call-done = f32[384,3072]{1,0:T(8,128)} async-done(((f32[1536,3072]{1,0:T(8,128)}), f32[384,3072]{1,0:T(8,128)}) %reduce-scatter.2.cloned.1.call-update) | async-done | bytes 4718608 | tf_op jit(solution)/shard_map/reduce_scatter | solution.py:93
  442.4 0.0 all-reduce.5.cloned.1.call-update
  442.4 1.2 copy-done.4
  443.6 0.4 copy-done.6
  444.0 0.4 copy-done.8
  444.3 10.0 %fusion.12 = (f32[1536]{0:T(1024)}, f32[384]{0:T(512)}, f32[384]{0:T(512)}, f32[1536]{0:T(1024)}, f32[384,1536]{1,0:T(8,128)}) fusion(bf16[384,1536]{1,0:T(8,128)(2,1)S(1)} %copy-done.4, f32[384]{0:T(512)S(1)} %add_rsqrt_fusion.1, f32[384]{0:T(512)S(1)} %broadcast_multiply_fusion.4, f32[1536]{0:T(1024)S(1)} %copy-done.11, ...), kind=kOutput, calls=%fused_computation.44 | convolution fusion | flops 3634491392 | bytes 15360000 | tf_op jit(solution)/shard_map/dot_general | solution.py:76
  454.3 39.7 %all-reduce = (f32[1536]{0:T(1024)}, f32[1536]{0:T(1024)}) all-reduce(f32[1536]{0:T(1024)} %get-tuple-element.42, f32[1536]{0:T(1024)} %get-tuple-element.45), channel_id=1, replica_groups=mesh['seq'=8,'fsdp'=4] {'seq','fsdp'}, use_global_device_ids=true, to_apply=%region_48.0 | all-reduce | flops 3072 | bytes 24576 | tf_op jit(solution)/shard_map/psum | solution.py:79
  494.0 0.7 broadcast_multiply_fusion.2
  494.7 3.4 fusion.11
  498.1 74.3 %all-reduce.7.cloned.1.call-done = f32[32,1536]{1,0:T(8,128)} async-done(((f32[32,1536]{1,0:T(8,128)}), f32[32,1536]{1,0:T(8,128)}) %all-reduce.7.cloned.1.call-update) | async-done | bytes 196624 | tf_op jit(solution)/shard_map/psum | solution.py:79
  572.4 174.5 %all-reduce.5.cloned.1.call-done = f32[384,3072]{1,0:T(8,128)} async-done(((f32[384,3072]{1,0:T(8,128)}), f32[384,3072]{1,0:T(8,128)}) %all-reduce.5.cloned.1.call-update) | async-done | bytes 4718608 | tf_op jit(solution)/shard_map/psum | solution.py:104
  746.9 5.1 copy.18
  752.0 0.7 copy.19
  (50 shorter events, 0.3 us)
Async XLA Ops:
  7.2 0.9 copy-start.10
  7.2 1.4 copy-start.2
  7.2 69.4 %copy-start.11 = (f32[1536]{0:T(1024)S(1)}, f32[1536]{0:T(1024)}, u32[]{:S(2)}) copy-start(f32[1536]{0:T(1024)} %param.9) | copy-start | bytes 18436
  7.2 69.4 %copy-start.12 = (f32[1536]{0:T(1024)S(1)}, f32[1536]{0:T(1024)}, u32[]{:S(2)}) copy-start(f32[1536]{0:T(1024)} %param.10) | copy-start | bytes 18436
  7.2 69.4 %all-gather.2.cloned.1.call-start = ((), (), s32[]{:S(2)}) async-start(), calls=%async_computation.1 | async-start | bytes 11796480 | tf_op jit(solution)/shard_map/all_gather | solution.py:30
  7.9 434.4 %reduce-scatter.2.cloned.1.call-start = ((), (), s32[]{:S(2)}) async-start(), calls=%async_computation.2 | async-start | bytes 23592960 | tf_op jit(solution)/shard_map/reduce_scatter | solution.py:93
  83.2 2.2 copy-start
  85.5 3.1 collective-permute-start
  99.1 86.1 %copy-start.13 = (f32[1536]{0:T(1024)S(1)}, f32[1536]{0:T(1024)}, u32[]{:S(2)}) copy-start(f32[1536]{0:T(1024)} %param.13) | copy-start | bytes 18436
  99.1 86.1 %copy-start.14 = (f32[1536]{0:T(1024)S(1)}, f32[1536]{0:T(1024)}, u32[]{:S(2)}) copy-start(f32[1536]{0:T(1024)} %param.14) | copy-start | bytes 18436
  229.9 0.6 copy-start.16
  229.9 8.9 %copy-start.15 = (f32[1536]{0:T(1024)}, f32[1536]{0:T(1024)S(1)}, u32[]{:S(2)}) copy-start(f32[1536]{0:T(1024)S(1)} %get-tuple-element.97) | copy-start | bytes 18436
  238.8 1.4 copy-start.1
  240.2 3.3 collective-permute-start.1
  283.9 4.5 copy-start.5
  283.9 5.5 copy-start.3
  288.4 1.0 copy-start.7
  298.8 273.6 %all-reduce.7.cloned.1.call-start = ((), (), s32[]{:S(2)}) async-start(), calls=%async_computation.4 | async-start | bytes 393216 | tf_op jit(solution)/shard_map/psum | solution.py:79
  307.6 439.3 %all-reduce.5.cloned.1.call-start = ((), (), s32[]{:S(2)}) async-start(), calls=%async_computation.3 | async-start | bytes 9437184 | tf_op jit(solution)/shard_map/psum | solution.py:104
  442.4 1.3 copy-start.4
  442.4 1.6 copy-start.6
  442.4 2.0 copy-start.8
  746.9 5.1 copy-start.9
Sparse Core Ops, SparseCore 0:
  9.6 66.9 all-gather.1
  298.9 143.3 reduce-scatter.1
  449.4 122.9 all-reduce.6
  576.3 170.5 all-reduce.4
where the time goes:
time: 760 us; the launch traced here: 759 us
  waiting for transfers between devices  454 us (60%)
  blocking collectives  164 us (22%)
  other arithmetic  80.9 us (11%)
  matrix products  26 us (3%)
  local copies, waits for them, and re-layouts  16.1 us (2%)
  between operations  14.2 us (2%)
    psum x1, waiting for transfers between devices, on_device(): grad_w_in = lax.psum(row_share, 'seq')  174 us
    reduce_scatter x1, waiting for transfers between devices, on_device(): lax.psum_scatter(lax.dot_general(normalized_rows, grad_hidden, (((0,), (0...  135 us
    psum x1, waiting for transfers between devices, on_device(): lax.psum((kernel_portion, jnp.sum(normalized_gradient * standardized_inpu...  74.3 us
    all_gather x1, waiting for transfers between devices, on_device(): full_weight = lax.all_gather(w_in, 'fsdp', axis=0, tiled=True)  67.3 us
    another operation x2, other arithmetic  44.8 us
    psum x1, blocking collectives, on_device(): lax.psum(jnp.sum(conv_out, axis=0), ('seq', 'fsdp')) / all_frames  44 us
    psum x1, blocking collectives, on_device(): lax.psum((jnp.sum(grad_z, axis=0), jnp.sum(grad_z * chat, axis=0)), ('seq...  40.2 us
    psum x1, blocking collectives, on_device(): lax.psum(jnp.sum(conv_centred * conv_centred, axis=0), ('seq', 'fsdp'))  40.1 us
  transfers between devices with their start and end apart: 6, of which 6 were waited for; matrix products, arithmetic and copies ran while one was open for 3% of the time, Pallas kernels for 0%

commit v1 on v0

--- a/solution.py
+++ b/solution.py
@@ -27,7 +27,13 @@
     )
     standardized_input = centered_rows * row_inverse_deviation
     normalized_rows = (standardized_input * layer_norm_gain + layer_norm_bias).astype(jnp.bfloat16)
-    full_weight = lax.all_gather(w_in, "fsdp", axis=0, tiled=True)
+    size = lax.axis_size("fsdp")
+    block_2, blocks = (w_in, [w_in])
+    for _ in range(size - 1):
+        block_2 = lax.ppermute(block_2, "fsdp", [(i_2, (i_2 + 1) % size) for i_2 in range(size)])
+        blocks.insert(0, block_2)
+    merged = jnp.concatenate(blocks, axis=0)
+    full_weight = jnp.roll(merged, (lax.axis_index("fsdp") + 1) * w_in.shape[0], axis=0)
     hidden = jnp.dot(normalized_rows, full_weight, preferred_element_type=jnp.float32)
     value_part = hidden[:, :features]
     gate_sig = jax.nn.sigmoid(hidden[:, features:])

time: 760 us -> 710 us (0.934)
  waiting for transfers between devices: 454 us -> 386 us
  local copies, waits for them, and re-layouts: 16.1 us -> 31.4 us
    ppermute x0 -> x3, waiting for transfers between devices: none -> 80.6 us  [on_device(): lax.ppermute(block_2, 'fsdp', [(i_2, (i_2 + 1) % size) for i_2 in range(s...]
    psum x1, waiting for transfers between devices: 74.3 us -> 0.01 us  [on_device(): lax.psum((kernel_portion, jnp.sum(normalized_gradient * standardized_inpu...]
    all_gather x1 -> x0, waiting for transfers between devices: 67.3 us -> none  [on_device(): full_weight = lax.all_gather(w_in, 'fsdp', axis=0, tiled=True)]
    unnamed x36 -> x45, local copies, waits for them, and re-layouts: 12.5 us -> 24.9 us
  transfers between devices with their start and end apart: 6 -> 8, of which waited for: 6 -> 6; matrix products, arithmetic and copies ran while one was open for 3% -> 4% of each run, Pallas kernels for 0% -> 0%
where the time goes in v1:
time: 710 us; the launch traced here: 709 us
  waiting for transfers between devices  386 us (54%)
  blocking collectives  165 us (23%)
  other arithmetic  83.2 us (12%)
  local copies, waits for them, and re-layouts  31.4 us (4%)
  matrix products  23.6 us (3%)
  between operations  16 us (2%)
    psum x1, waiting for transfers between devices, on_device(): grad_w_in = lax.psum(row_share, 'seq')  168 us
    reduce_scatter x1, waiting for transfers between devices, on_device(): lax.psum_scatter(lax.dot_general(normalized_rows, grad_hidden, (((0,), (0...  135 us
    ppermute x3, waiting for transfers between devices, on_device(): lax.ppermute(block_2, 'fsdp', [(i_2, (i_2 + 1) % size) for i_2 in range(s...  80.6 us
    psum x1, blocking collectives, on_device(): lax.psum(jnp.sum(conv_out, axis=0), ('seq', 'fsdp')) / all_frames  44.6 us
    another operation x2, other arithmetic  44.6 us
    psum x1, blocking collectives, on_device(): lax.psum(jnp.sum(conv_centred * conv_centred, axis=0), ('seq', 'fsdp'))  40.6 us
    psum x1, blocking collectives, on_device(): lax.psum((jnp.sum(grad_z, axis=0), jnp.sum(grad_z * chat, axis=0)), ('seq...  39.8 us
    psum x1, blocking collectives, on_device(): lax.psum((kernel_portion, jnp.sum(normalized_gradient * standardized_inpu...  39.7 us
  transfers between devices with their start and end apart: 8, of which 6 were waited for; matrix products, arithmetic and copies ran while one was open for 4% of the time, Pallas kernels for 0%

profile of v1, /device:TPU:0, one launch (start us, length us, event | category | flops | bytes accessed | tf_op | source)
XLA Modules:
  0.0 708.8 jit_solution(8734003535897168089)
XLA Ops:
  8.0 0.0 reduce-scatter.2.cloned.1.call-start
  8.0 0.5 collective-permute-start
  8.5 28.7 %collective-permute-done = bf16[384,3072]{1,0:T(8,128)(2,1)S(1)} collective-permute-done((bf16[384,3072]{1,0:T(8,128)(2,1)}, bf16[384,3072]{1,0:T(8,128)(2,1)S(1)}, u32[]{:S(2)}, u32[]{:S(2)}) %collective-permute-start) | collective-permute-done | bytes 2359328 | tf_op jit(solution)/shard_map/ppermute | solution.py:33
  37.2 0.0 collective-permute-start.1
  37.3 28.3 %collective-permute-done.1 = bf16[384,3072]{1,0:T(8,128)(2,1)} collective-permute-done((bf16[384,3072]{1,0:T(8,128)(2,1)S(1)}, bf16[384,3072]{1,0:T(8,128)(2,1)}, u32[]{:S(2)}, u32[]{:S(2)}) %collective-permute-start.1) | collective-permute-done | bytes 2359328 | tf_op jit(solution)/shard_map/ppermute | solution.py:33
  65.6 1.8 slice_reduce_fusion.31
  67.4 1.5 convert_reduce_fusion
  68.9 1.7 fusion.17
  70.6 23.6 %collective-permute-done.2 = bf16[384,3072]{1,0:T(8,128)(2,1)} collective-permute-done((bf16[384,3072]{1,0:T(8,128)(2,1)}, bf16[384,3072]{1,0:T(8,128)(2,1)}, u32[]{:S(2)}, u32[]{:S(2)}) %collective-permute-start.2) | collective-permute-done | bytes 2359328 | tf_op jit(solution)/shard_map/ppermute | solution.py:33
  94.2 1.8 constant_dynamic-update-slice_fusion.7
  96.0 1.8 constant_dynamic-update-slice_fusion.6
  97.8 0.0 copy-start.5
  97.8 0.2 constant_dynamic-update-slice_fusion.5
  98.0 1.5 copy-done.5
  99.5 0.2 constant_dynamic-update-slice_fusion.4
  99.6 1.8 constant_dynamic-update-slice_fusion.3
  101.5 1.8 constant_dynamic-update-slice_fusion.2
  103.3 0.2 constant_dynamic-update-slice_fusion.1
  103.4 0.0 copy-start.2
  103.5 0.0 copy-start.12
  103.5 0.0 copy-start.13
  103.5 0.2 constant_dynamic-update-slice_fusion
  103.6 1.1 copy-done.2
  104.7 4.2 fusion.2
  108.9 2.3 copy-done.10
  111.2 0.6 multiply_convert_fusion.3
  111.8 1.6 copy-done
  113.4 1.8 collective-permute-start.3
  115.3 1.6 slice_reduce_fusion.30
  116.8 0.3 maximum_convert_fusion
  117.2 10.2 %fusion.123 = (f32[1536]{0:T(1024)S(1)}, f32[384,1536]{1,0:T(8,128)}) fusion(f32[415,1536]{1,0:T(8,128)S(1)} %maximum_convert_fusion, f32[1536]{0:T(1024)S(1)} %get-tuple-element.76, f32[1536]{0:T(1024)S(1)} %get-tuple-element.77, f32[1536]{0:T(1024)S(1)} %get-tuple-element.47, f32[1536]{0:T(1024)S(1)} %get-tuple-element.48, ...), kind=kLoop, calls=%fused_computation.273 | loop fusion | flops 37747200 | bytes 78059520 | tf_op jit(solution)/shard_map/reduce_sum | solution.py:50
  127.4 44.6 %psum.56 = f32[1536]{0:T(1024)S(1)} all-reduce(f32[1536]{0:T(1024)S(1)} %get-tuple-element.85), channel_id=1, replica_groups=mesh['seq'=8,'fsdp'=4] {'seq','fsdp'}, use_global_device_ids=true, to_apply=%region_3.4 | all-reduce | flops 1536 | bytes 12288 | tf_op jit(solution)/shard_map/psum | solution.py:50
  172.0 1.9 multiply_reduce_fusion.33
  173.9 40.6 %psum.57 = f32[1536]{0:T(1024)S(1)} all-reduce(f32[1536]{0:T(1024)S(1)} %multiply_reduce_fusion.33), channel_id=1, replica_groups=mesh['seq'=8,'fsdp'=4] {'seq','fsdp'}, use_global_device_ids=true, to_apply=%region_5.6 | all-reduce | flops 1536 | bytes 12288 | tf_op jit(solution)/shard_map/psum | solution.py:52
  214.5 4.5 fusion.121
  219.0 39.8 %all-reduce.1 = (f32[1536]{0:T(1024)S(1)}, f32[1536]{0:T(1024)S(1)}) all-reduce(f32[1536]{0:T(1024)S(1)} %get-tuple-element.41, f32[1536]{0:T(1024)S(1)} %get-tuple-element.40), channel_id=1, replica_groups=mesh['seq'=8,'fsdp'=4] {'seq','fsdp'}, use_global_device_ids=true, to_apply=%region_9.10 | all-reduce | flops 3072 | bytes 24576 | tf_op jit(solution)/shard_map/psum | solution.py:59
  258.8 0.6 copy-done.17
  259.4 8.2 %multiply_reduce_fusion = (f32[1536]{0:T(1024)S(1)}, f32[1536]{0:T(1024)S(1)}, f32[1536]{0:T(1024)S(1)}, f32[1536]{0:T(1024)S(1)}, f32[1536]{0:T(1024)S(1)}, /*i...) fusion(f32[415,1536]{1,0:T(8,128)S(1)} %maximum_convert_fusion,, ...), kind=kLoop, calls=%fused_computation.173 | loop fusion | flops 31822848 | bytes 48519168 | tf_op jit(solution)/shard_map/reduce_sum | solution.py:72
  267.7 1.4 copy-done.1
  269.1 1.3 collective-permute-start.4
  270.4 2.0 collective-permute-done.4
  272.5 40.1 %multiply_convert_fusion.1 = (bf16[384,1536]{1,0:T(8,128)(2,1)S(1)}, f32[384,1536]{1,0:T(8,128)}) fusion(f32[384,3072]{1,0:T(8,128)} %copy-done, f32[31,1536]{1,0:T(8,128)S(1)} %collective-permute-done.4, f32[384,1536]{1,0:T(8,128)} %copy-done.1, f32[1536]{0:T(1024)S(1)} %get-tuple-element.76, f32[1536]{0:T(1024)S(1)} %get-tuple-element.77, ...), kind=kLoop, calls=%fused_computation.206 | loop fusion | flops 58392576 | bytes 8644608 | tf_op jit(solution)/shard_map/convert
  312.6 0.0 copy-start.3
  312.6 4.4 multiply_convert_fusion
  317.1 1.0 copy-done.8
  318.1 9.3 %fusion.113 = f32[1536,3072]{1,0:T(8,128)} fusion(bf16[384,1536]{1,0:T(8,128)(2,1)S(1)} %multiply_convert_fusion, bf16[384,1536]{1,0:T(8,128)(2,1)S(1)} %get-tuple-element.83, bf16[384,1536]{1,0:T(8,128)(2,1)S(1)} %copy-done.3, f32[1536]{0:T(1024)S(1)} %copy-done.13, f32[1536]{0:T(1024)S(1)} %copy-done.12, f32[384]{0:T(512)S(1)} %add_rsqrt_fusion.1, ...), kind=kOutput, calls=%fused_computation.218 | convolution fusion | flops 3632136192 | bytes 22428672 | tf_op jit(solution)/shard_map/dot_general | solution.py:100
  327.4 0.0 reduce-scatter.2.cloned.1.call-update
  327.5 0.3 all-reduce.7.cloned.1.call-start
  327.7 5.4 multiply_reduce_fusion.18
  333.6 2.8 stack.131
  336.4 0.0 all-reduce.7.cloned.1.call-update
  336.4 0.0 all-reduce.5.cloned.1.call-start
  336.5 135.1 %reduce-scatter.2.cloned.1.call-done = f32[384,3072]{1,0:T(8,128)} async-done(((f32[1536,3072]{1,0:T(8,128)}), f32[384,3072]{1,0:T(8,128)}) %reduce-scatter.2.cloned.1.call-update) | async-done | bytes 4718608 | tf_op jit(solution)/shard_map/reduce_scatter | solution.py:99
  471.6 0.0 all-reduce.5.cloned.1.call-update
  471.7 1.2 copy-done.4
  472.9 0.4 copy-done.7
  473.3 0.4 copy-done.9
  473.6 10.0 %fusion.16 = (f32[1536]{0:T(1024)}, f32[384]{0:T(512)}, f32[384]{0:T(512)}, f32[1536]{0:T(1024)}, f32[384,1536]{1,0:T(8,128)}) fusion(bf16[384,1536]{1,0:T(8,128)(2,1)S(1)} %copy-done.4, f32[384]{0:T(512)S(1)} %add_rsqrt_fusion.1, f32[384]{0:T(512)S(1)} %broadcast_multiply_fusion.4, f32[1536]{0:T(1024)S(1)} %copy-done.12, ...), kind=kOutput, calls=%fused_computation.48 | convolution fusion | flops 3634491392 | bytes 15360004 | tf_op jit(solution)/shard_map/dot_general | solution.py:82
  483.6 39.7 %all-reduce = (f32[1536]{0:T(1024)}, f32[1536]{0:T(1024)}) all-reduce(f32[1536]{0:T(1024)} %get-tuple-element.42, f32[1536]{0:T(1024)} %get-tuple-element.45), channel_id=1, replica_groups=mesh['seq'=8,'fsdp'=4] {'seq','fsdp'}, use_global_device_ids=true, to_apply=%region_48.49 | all-reduce | flops 3072 | bytes 24576 | tf_op jit(solution)/shard_map/psum | solution.py:85
  523.3 0.7 broadcast_multiply_fusion.2
  524.0 3.4 fusion.15
  527.5 168.2 %all-reduce.5.cloned.1.call-done = f32[384,3072]{1,0:T(8,128)} async-done(((f32[384,3072]{1,0:T(8,128)}), f32[384,3072]{1,0:T(8,128)}) %all-reduce.5.cloned.1.call-update) | async-done | bytes 4718608 | tf_op jit(solution)/shard_map/psum | solution.py:110
  695.6 5.1 copy.25
  700.7 0.7 copy.26
  (63 shorter events, 0.3 us)
Async XLA Ops:
  8.0 463.6 %reduce-scatter.2.cloned.1.call-start = ((), (), s32[]{:S(2)}) async-start(), calls=%async_computation.1 | async-start | bytes 23592960 | tf_op jit(solution)/shard_map/reduce_scatter | solution.py:99
  8.0 29.2 %collective-permute-start = (bf16[384,3072]{1,0:T(8,128)(2,1)}, bf16[384,3072]{1,0:T(8,128)(2,1)S(1)}, u32[]{:S(2)}, u32[]{:S(2)}) collective-permute-start(bf16[384,3072]{1,0:T(8,128)(2,1)} %param.11), channel_id=1, source_target_pairs={{0,1},{1,2},{2,3},{3,0},{4,5},{5,6},{6,7},{7,4},{8,9},{9,10},{10,1... | collective-permute-start | bytes 7077896 | tf_op jit(solution)/shard_map/ppermute | solution.py:33
  37.2 28.4 %collective-permute-start.1 = (bf16[384,3072]{1,0:T(8,128)(2,1)S(1)}, bf16[384,3072]{1,0:T(8,128)(2,1)}, u32[]{:S(2)}, u32[]{:S(2)}) collective-permute-start(bf16[384,3072]{1,0:T(8,128)(2,1)S(1)} %collective-permute-done), channel_id=1, source_target_pairs={{0,1},{1,2},{2,3},{3,0},{4,5},{5,6},{6,7},{7,4},{8,9},{9,10},{10,1... | collective-permute-start | bytes 7077896 | tf_op jit(solution)/shard_map/ppermute | solution.py:33
  65.6 28.6 %collective-permute-start.2 = (bf16[384,3072]{1,0:T(8,128)(2,1)}, bf16[384,3072]{1,0:T(8,128)(2,1)}, u32[]{:S(2)}, u32[]{:S(2)}) collective-permute-start(bf16[384,3072]{1,0:T(8,128)(2,1)} %collective-permute-done.1), channel_id=1, source_target_pairs={{0,1},{1,2},{2,3},{3,0},{4,5},{5,6},{6,7},{7,4},{8,9},{9,10},{10,1... | collective-permute-start | bytes 7077896 | tf_op jit(solution)/shard_map/ppermute | solution.py:33
  97.8 1.7 copy-start.5
  103.4 1.3 copy-start.2
  103.5 1.3 copy-start.12
  103.5 1.3 copy-start.13
  104.7 6.5 copy-start.10
  111.2 2.2 copy-start
  113.4 3.4 collective-permute-start.3
  127.4 87.1 %copy-start.14 = (f32[1536]{0:T(1024)S(1)}, f32[1536]{0:T(1024)}, u32[]{:S(2)}) copy-start(f32[1536]{0:T(1024)} %param.13) | copy-start | bytes 18436
  127.4 87.1 %copy-start.15 = (f32[1536]{0:T(1024)S(1)}, f32[1536]{0:T(1024)}, u32[]{:S(2)}) copy-start(f32[1536]{0:T(1024)} %param.14) | copy-start | bytes 18436
  258.8 0.6 copy-start.17
  258.8 8.9 %copy-start.16 = (f32[1536]{0:T(1024)}, f32[1536]{0:T(1024)S(1)}, u32[]{:S(2)}) copy-start(f32[1536]{0:T(1024)S(1)} %get-tuple-element.97) | copy-start | bytes 18436
  267.7 1.4 copy-start.1
  269.1 3.3 collective-permute-start.4
  312.6 4.5 copy-start.6
  312.6 5.5 copy-start.3
  317.1 1.0 copy-start.8
  327.5 200.0 %all-reduce.7.cloned.1.call-start = ((), (), s32[]{:S(2)}) async-start(), calls=%async_computation.3 | async-start | bytes 393216 | tf_op jit(solution)/shard_map/psum | solution.py:85
  336.4 359.2 %all-reduce.5.cloned.1.call-start = ((), (), s32[]{:S(2)}) async-start(), calls=%async_computation.2 | async-start | bytes 9437184 | tf_op jit(solution)/shard_map/psum | solution.py:110
  471.6 1.3 copy-start.4
  471.6 1.6 copy-start.7
  471.6 2.0 copy-start.9
  695.6 5.1 copy-start.11
Sparse Core Ops, SparseCore 0:
  327.6 144.0 reduce-scatter.1
Sparse Core Ops, SparseCore 1:
  336.5 185.0 all-reduce.6
  525.5 170.0 all-reduce.4
